TPU v7x, 128 devices: a whole 4x4x4 slice. The times are simulated.
128 devices in a mesh: pipe: 8 (over z, core), ctx: 16 (over y, x).
Axes of the slice: x: 4, y: 4, z: 4, core: 2. Of those that a mesh axis runs over, the one named last changes fastest.
Arguments:
- grad_in: bfloat16 [8, 4096, 8192], P('pipe', 'ctx'), may hold values from -6 to 6
- query: bfloat16 [8, 4096, 512], P('pipe', 'ctx'), may hold values from -8 to 8
- keyval: bfloat16 [8, 4096, 256], P('pipe', 'ctx'), may hold values from -8 to 8
- w_qkv: bfloat16 [8, 8192, 768], P('pipe', 'ctx'), may hold values from -0.0625 to 0.0625
- w_out: bfloat16 [8, 8192, 512], P('pipe', 'ctx'), may hold values from -0.25 to 0.25
- doc_lengths: int32 [8, 8], P('pipe'), may hold values from 1 to 2048, 4096 in all within a row
- order: int32 [8, 32], P('pipe'), may hold values from 0 to 31, as said below
Outputs:
- passed_grad: bfloat16 [8, 4096, 8192], P('pipe', 'ctx')
Inputs may be any that keep to these rules, and one draw needn't show every extreme that they name: Each row of order is a permutation of 0 to 31; entry d * 2 + k (device d's stored slot k, k < 2) names one of the sequence blocks e * 2 to e * 2 + 1 of device e = (d + k * 8) mod 16. `doc_lengths`: each row sums to 4096 and its largest entry is 2048.
All inputs are finite; a program needn't handle non-finite values.
Results may differ from a plain program's by a relative error of at most 0.015.
Values may be sent and summed in bfloat16 or wider, within the bound.
No kernel may reach another device: no remote copies, remote signals or barrier semaphores. Data moves between devices by JAX's collectives and lax.ppermute only.
A program may use at most 128 MiB of HBM per device.

v0:
```python
import math
import jax
import jax.numpy as jnp
from jax import lax
from jax.sharding import PartitionSpec as P

BLOCK = 128
ROPE_BASE = 500000.0
MASKED = -1e30


def passed_along(value, axis, steps):
    count = lax.axis_size(axis)
    pairs = [(source, (source + steps) % count) for source in range(count)]
    return lax.ppermute(value, axis, pairs)


def passed_along_2(value, axis, by):
    size = lax.axis_size(axis)
    pairs = [(i, i + by) for i in range(size) if 0 <= i + by < size]
    return lax.ppermute(value, axis, pairs)


def rope_tables(positions, head_dim):
    half_width = head_dim // 2
    inv_freq = ROPE_BASE ** (-(jnp.arange(half_width, dtype=jnp.float32) * 2.0 / head_dim))
    angles = positions.astype(jnp.float32)[:, None] * inv_freq[None, :]
    angles = jnp.concatenate([angles, angles], axis=1)
    return (jnp.cos(angles), jnp.sin(angles))


def unrotate(gradient, positions):
    cosine, sine_table = rope_tables(positions, gradient.shape[1])
    half_width = gradient.shape[1] // 2
    turned = jnp.concatenate([-gradient[:, half_width:], gradient[:, :half_width]], axis=1)
    return gradient * cosine - turned * sine_table


def doc_ids(positions, lengths):
    doc_ends = jnp.cumsum(lengths)[:-1]
    return jnp.sum((positions[:, None] >= doc_ends[None, :]).astype(jnp.int32), axis=1)


def seq_to_stored(rows, block_order, device, ctx_size, per_device):
    width = rows.shape[1]
    first_block = device * per_device
    blocks = rows.reshape(per_device, BLOCK, width)
    pieces = []
    for slot_k in range(per_device):
        offset = slot_k * ctx_size // per_device
        slot_at = (device - offset) % ctx_size * per_device + slot_k
        local_index = block_order[slot_at] - first_block
        chosen = lax.dynamic_index_in_dim(blocks, local_index, 0, keepdims=False)
        if slot_k > 0:
            chosen = passed_along(chosen, "ctx", -offset)
        pieces.append(chosen)
    return jnp.concatenate(pieces, axis=0)


def stored_to_seq(rows, block_order, device, ctx_size, per_device):
    width = rows.shape[1]
    first_block = device * per_device
    blocks = rows.reshape(per_device, BLOCK, width)
    pieces = []
    local_ids = []
    for slot_k in range(per_device):
        offset = slot_k * ctx_size // per_device
        piece = blocks[slot_k]
        if slot_k > 0:
            piece = passed_along(piece, "ctx", offset)
        pieces.append(piece)
        sender_slot = (device - offset) % ctx_size * per_device + slot_k
        local_ids.append(block_order[sender_slot] - first_block)
    stacked = jnp.stack(pieces)
    index_list = jnp.stack(local_ids)
    choose = (jnp.arange(per_device, dtype=jnp.int32)[:, None] == index_list[None, :]).astype(
        rows.dtype
    )
    placed = jnp.einsum("pk,kbw->pbw", choose, stacked, preferred_element_type=jnp.float32)
    return placed.astype(rows.dtype).reshape(-1, width)


def contract_rows(left_rows, right_rows):
    return lax.dot_general(
        left_rows, right_rows, (((0,), (0,)), ((), ())), preferred_element_type=jnp.float32
    )


def contract_cols(left_rows, right_rows):
    return lax.dot_general(
        left_rows, right_rows, (((1,), (1,)), ((), ())), preferred_element_type=jnp.float32
    )


def block_scores(query_rows, key_rows, query_pos, query_doc, key_pos, key_doc, score_scale):
    scores = contract_cols(query_rows, key_rows) * score_scale
    visible = (query_doc[:, None] == key_doc[None, :]) & (key_pos[None, :] <= query_pos[:, None])
    return (scores, visible)


def body(grad_in, query, keyval, w_qkv, w_out, doc_lengths, order):
    section_grad_in = grad_in[0]
    stored_query = query[0]
    stored_keyval = keyval[0]
    in_weight = w_qkv[0]
    out_weight = w_out[0]
    lengths = doc_lengths[0]
    block_order = order[0]
    ctx_size = lax.axis_size("ctx")
    device = lax.axis_index("ctx")
    local_rows = section_grad_in.shape[0]
    head_dim = stored_keyval.shape[1] // 2
    group = stored_query.shape[1] // head_dim
    per_device = local_rows // BLOCK
    block_count = block_order.shape[0]
    seq_len = local_rows * ctx_size
    first_row = device * local_rows
    score_scale = 1.0 / math.sqrt(head_dim)
    key_block = math.gcd(seq_len, 512)
    key_steps = seq_len // key_block
    within = jnp.arange(BLOCK, dtype=jnp.int32)
    out_grad = jnp.dot(
        section_grad_in,
        lax.all_gather(out_weight, "ctx", axis=0, tiled=True),
        preferred_element_type=jnp.float32,
    ).astype(jnp.bfloat16)
    local_out_grad = seq_to_stored(out_grad, block_order, device, ctx_size, per_device)
    query_positions = (block_order[:, None] * BLOCK + within[None, :]).reshape(-1)
    gathered = lax.all_gather(stored_keyval, "ctx", axis=0, tiled=True)
    slot_ids = jnp.arange(block_count, dtype=jnp.int32)
    inverse = jnp.sum(
        jnp.where(block_order[None, :] == slot_ids[:, None], slot_ids[None, :], 0), axis=1
    )
    all_keyval = gathered.reshape(block_count, BLOCK, 2 * head_dim)[inverse].reshape(
        seq_len, 2 * head_dim
    )
    key_positions = jnp.arange(seq_len, dtype=jnp.int32)
    key_docs = doc_ids(key_positions, lengths)
    query_pos = lax.dynamic_slice_in_dim(query_positions, first_row, local_rows)
    query_doc = doc_ids(query_pos, lengths)
    flat_rows = local_rows * group
    flat_query = stored_query.reshape(flat_rows, head_dim)
    flat_grad = local_out_grad.reshape(flat_rows, head_dim)
    flat_pos = jnp.repeat(query_pos, group)
    flat_doc = jnp.repeat(query_doc, group)
    key_blocks = (
        all_keyval.reshape(key_steps, key_block, 2 * head_dim),
        key_positions.reshape(key_steps, key_block),
        key_docs.reshape(key_steps, key_block),
    )

    def running_total(carried, current):
        row_top, row_total, weighted = carried
        pair_rows, key_pos, key_doc = current
        scores, visible = block_scores(
            flat_query, pair_rows[:, :head_dim], flat_pos, flat_doc, key_pos, key_doc, score_scale
        )
        new_top = jnp.maximum(row_top, jnp.max(jnp.where(visible, scores, MASKED), axis=1))
        rescale = jnp.exp(row_top - new_top)
        weights = jnp.where(visible, jnp.exp(scores - new_top[:, None]), 0.0)
        row_total = row_total * rescale + jnp.sum(weights, axis=1)
        value_wide = pair_rows[:, head_dim:].astype(jnp.float32)
        weighted = weighted * rescale[:, None] + jnp.dot(
            weights, value_wide, precision=lax.Precision.HIGHEST
        )
        return ((new_top, row_total, weighted), None)

    start_top = jnp.full((flat_rows,), MASKED, jnp.float32)
    start_carry = (
        start_top,
        jnp.zeros((flat_rows,), jnp.float32),
        jnp.zeros((flat_rows, head_dim), jnp.float32),
    )
    (row_top, row_total, weighted), unused = lax.scan(running_total, start_carry, key_blocks)
    log_total = row_top + jnp.log(row_total)
    attn_out = weighted / row_total[:, None]
    row_delta = jnp.sum(flat_grad.astype(jnp.float32) * attn_out, axis=1)

    def grad_step(summed, current):
        pair_rows, key_pos, key_doc = current
        scores, visible = block_scores(
            flat_query, pair_rows[:, :head_dim], flat_pos, flat_doc, key_pos, key_doc, score_scale
        )
        attn_prob = jnp.where(visible, jnp.exp(scores - log_total[:, None]), 0.0)
        prob_grad = contract_cols(flat_grad, pair_rows[:, head_dim:])
        score_grad = (score_scale * attn_prob * (prob_grad - row_delta[:, None])).astype(
            jnp.bfloat16
        )
        summed = summed + jnp.dot(
            score_grad, pair_rows[:, :head_dim], preferred_element_type=jnp.float32
        )
        key_term = contract_rows(score_grad, flat_query)
        value_term = contract_rows(attn_prob.astype(jnp.bfloat16), flat_grad)
        return (summed, jnp.concatenate([key_term, value_term], axis=1))

    query_grad_rot, key_terms = lax.scan(
        grad_step, jnp.zeros((flat_rows, head_dim), jnp.float32), key_blocks
    )
    own_positions = first_row + jnp.arange(local_rows, dtype=jnp.int32)
    keyval_grad = lax.psum_scatter(
        key_terms.reshape(seq_len, 2 * head_dim).astype(jnp.bfloat16),
        "ctx",
        scatter_dimension=0,
        tiled=True,
    ).astype(jnp.float32)
    query_grad = (
        unrotate(query_grad_rot, flat_pos)
        .reshape(local_rows, group * head_dim)
        .astype(jnp.bfloat16)
    )
    query_grad = stored_to_seq(query_grad, block_order, device, ctx_size, per_device)
    key_grad = unrotate(keyval_grad[:, :head_dim], own_positions).astype(jnp.bfloat16)
    value_grad = keyval_grad[:, head_dim:].astype(jnp.bfloat16)
    qkv_grad = jnp.concatenate([query_grad, key_grad, value_grad], axis=1)
    projected = contract_cols(qkv_grad, lax.all_gather(in_weight, "ctx", axis=0, tiled=True))
    section_grad = (section_grad_in.astype(jnp.float32) + projected).astype(jnp.bfloat16)
    passed = passed_along_2(section_grad, "pipe", -1)
    return passed[None]


def solution(mesh):
    return jax.shard_map(
        body,
        mesh=mesh,
        in_specs=(
            P("pipe", "ctx", None),
            P("pipe", "ctx", None),
            P("pipe", "ctx", None),
            P("pipe", "ctx", None),
            P("pipe", "ctx", None),
            P("pipe", None),
            P("pipe", None),
        ),
        out_specs=P("pipe", "ctx", None),
        check_vma=False,
    )
```

profile of v0, /device:TPU:1, one launch (start us, length us, event | category | flops | bytes accessed | tf_op | source)
XLA Modules:
  0.0 424.1 jit_solution(3476864368131219313)
XLA Ops:
  8.1 1.3 constant_dynamic-slice_fusion.5
  11.6 1.1 reshape_squeeze.3
  14.5 42.2 %all-gather.7.cloned.1.call-done = bf16[1,4096,256]{2,1,0:T(8,128)(2,1)} async-done(((bf16[1,256,256]{2,1,0:T(8,128)(2,1)}), bf16[1,4096,256]{2,1,0:T(8,128)(2,1)}) %all-gather.7.cloned.1.call-update) | async-done | bytes 2097168 | tf_op jit(solution)/shard_map/all_gather | solution.py:129
  56.7 3.6 gather_fusion
  60.3 51.0 %while.28 = (s32[]{:T(128)}, f32[1024]{0:T(1024)S(1)}, f32[1024]{0:T(1024)S(1)}, f32[1024,128]{1,0:T(8,128)}, s32[8,512]{1,0:T(8,128)S(1)}, /*index=5*/s32[8,512...) while((s32[]{:T(128)}, f32[1024]{0:T(1024)S(1)}, ...), condition=%wide.region_7.8_spmd.clone, body=%wide.region_4.7_spmd.clone.sunk | while | flops 949883904 | bytes 12720321 | solution.py:174
  60.3 1.0 dynamic-slice_bitcast_fusion.6
  63.4 2.4 convolution_add_fusion.4
  69.8 2.4 convolution_add_fusion.4
  73.1 1.0 dynamic-slice_bitcast_fusion.6
  76.2 2.4 convolution_add_fusion.4
  82.6 2.4 convolution_add_fusion.4
  85.8 1.0 dynamic-slice_bitcast_fusion.6
  88.9 2.4 convolution_add_fusion.4
  92.2 1.1 dynamic-slice_bitcast_fusion.6
  95.3 2.4 convolution_add_fusion.4
  101.7 2.4 convolution_add_fusion.4
  104.9 1.0 dynamic-slice_bitcast_fusion.6
  108.0 2.4 convolution_add_fusion.4
  111.3 18.4 %all-gather.9.cloned.1.call-done = bf16[1,8192,512]{2,1,0:T(8,128)(2,1)} async-done(((bf16[1,512,512]{2,1,0:T(8,128)(2,1)}), bf16[1,8192,512]{2,1,0:T(8,128)(2,1)}) %all-gather.9.cloned.1.call-update) | async-done | bytes 8388624 | tf_op jit(solution)/shard_map/all_gather | solution.py:124
  129.7 7.0 %fusion.43 = bf16[256,512]{1,0:T(8,128)(2,1)S(1)} fusion(bf16[1,8192,512]{2,1,0:T(8,128)(2,1)} %all-gather.9.cloned.1.call-done, bf16[1,256,8192]{2,1,0:T(8,128)(2,1)} %param.11), kind=kOutput, calls=%fused_computation.55 | convolution fusion | flops 2147614720 | bytes 12845056 | tf_op jit(solution)/shard_map/dot_general | solution.py:122
  136.7 2.8 collective-permute-start
  139.5 3.2 collective-permute-done
  143.3 41.0 %while.29 = (s32[]{:T(128)}, f32[1024,128]{1,0:T(8,128)S(1)}, bf16[8,512,256]{2,1,0:T(8,128)(2,1)}, s32[8,512]{1,0:T(8,128)S(1)}, s32[8,512]{1,0:T(8,128)S(1)}, ...) while((s32[]{:T(128)}, f32[1024,128]{1,0:T(8,128)S(1)}, ...), condition=%wide.region_10.11_spmd.clone, body=%wide.region_9.10_spmd.clone.sunk | while | flops 677642240 | bytes 14342807 | solution.py:196
  185.6 2.4 fusion.49
  188.1 2.9 collective-permute-start.1
  191.2 2.4 collective-permute-done.1
  194.6 63.0 %reduce-scatter.2.cloned.1.call-done = bf16[256,256]{1,0:T(8,128)(2,1)} async-done(((bf16[4096,256]{1,0:T(8,128)(2,1)}), bf16[256,256]{1,0:T(8,128)(2,1)}) %reduce-scatter.2.cloned.1.call-update) | async-done | bytes 131088 | tf_op jit(solution)/shard_map/reduce_scatter | solution.py:200
  260.9 89.8 %all-gather.11.cloned.1.call-done = bf16[1,8192,768]{2,1,0:T(8,128)(2,1)} async-done(((bf16[1,512,768]{2,1,0:T(8,128)(2,1)}), bf16[1,8192,768]{2,1,0:T(8,128)(2,1)}) %all-gather.11.cloned.1.call-update) | async-done | bytes 12582928 | tf_op jit(solution)/shard_map/all_gather | solution.py:215
  350.7 14.8 %fusion.37 = bf16[256,8192]{1,0:T(8,128)(2,1)} fusion(bf16[1,8192,768]{2,1,0:T(8,128)(2,1)} %all-gather.11.cloned.1.call-done, bf16[1,256,8192]{2,1,0:T(8,128)(2,1)} %param.11, bf16[256,128]{1,0:T(8,128)(2,1)S(1)} %slice.80, bf16[256,128]{1,0:T(8,128)(2,1)S(1)} %fusion.57, bf16[256,512]{1,0:T(8,128)(2,1)S(1)} %bitcast.123), kind=kOutput, calls=%fused_computation.50 | convolution fusion | flops 3228696576 | bytes 21364736 | tf_op jit(solution)/shard_map/dot_general | solution.py:90
  365.5 2.6 collective-permute-start.2
  368.1 47.5 %collective-permute-done.2 = bf16[256,8192]{1,0:T(8,128)(2,1)S(1)} collective-permute-done((bf16[256,8192]{1,0:T(8,128)(2,1)}, bf16[256,8192]{1,0:T(8,128)(2,1)S(1)}, u32[]{:S(2)}, u32[]{:S(2)}) %collective-permute-start.2) | collective-permute-done | bytes 4194336 | tf_op jit(solution)/shard_map/ppermute | solution.py:21
  415.6 2.0 copy.44
  (278 shorter events, 76.7 us)
Async XLA Ops:
  6.5 50.2 %all-gather.7.cloned.1.call-start = ((), (), s32[]{:S(2)}) async-start(), calls=%async_computation.2 | async-start | bytes 2228224 | tf_op jit(solution)/shard_map/all_gather | solution.py:129
  7.3 122.5 %all-gather.9.cloned.1.call-start = ((), (), s32[]{:S(2)}) async-start(), calls=%async_computation.3 | async-start | bytes 8912896 | tf_op jit(solution)/shard_map/all_gather | solution.py:124
  8.0 249.6 %reduce-scatter.2.cloned.1.call-start = ((), (), s32[]{:S(2)}) async-start(), calls=%async_computation.1 | async-start | bytes 2228224 | tf_op jit(solution)/shard_map/reduce_scatter | solution.py:200
  62.4 1.0 copy-start
  65.9 0.8 copy-start.1
  68.8 1.1 copy-start
  72.3 0.8 copy-start.1
  75.1 1.1 copy-start
  78.6 0.8 copy-start.1
  81.5 1.0 copy-start
  85.0 0.8 copy-start.1
  87.9 1.0 copy-start
  91.3 0.8 copy-start.1
  94.3 1.0 copy-start
  97.8 0.8 copy-start.1
  100.6 1.0 copy-start
  104.1 0.8 copy-start.1
  107.0 1.0 copy-start
  110.5 0.8 copy-start.1
  111.3 31.6 %copy-start.2 = (f32[1024,128]{1,0:T(8,128)S(1)}, f32[1024,128]{1,0:T(8,128)}, u32[]{:S(2)}) copy-start(f32[1024,128]{1,0:T(8,128)} %get-tuple-element.124) | copy-start | bytes 1572868
  136.7 5.9 %collective-permute-start = (bf16[128,512]{1,0:T(8,128)(2,1)S(1)}, bf16[128,512]{1,0:T(8,128)(2,1)S(1)}, u32[]{:S(2)}, u32[]{:S(2)}) collective-permute-start(bf16[128,512]{1,0:T(8,128)(2,1)S(1)} %get-tuple-element.270), channel_id=1, source_target_pairs={{0,8},{1,9},{2,10},{3,11},{4,12},{5,13},{6,14},{7,15},{8,0},{9,1},... | collective-permute-start | bytes 393224 | tf_op jit(solution)/shard_map/ppermute | solution.py:15
  184.3 166.3 %all-gather.11.cloned.1.call-start = ((), (), s32[]{:S(2)}) async-start(), calls=%async_computation.4 | async-start | bytes 13369344 | tf_op jit(solution)/shard_map/all_gather | solution.py:215
  188.1 5.6 %collective-permute-start.1 = (bf16[128,512]{1,0:T(8,128)(2,1)S(1)}, bf16[128,512]{1,0:T(8,128)(2,1)S(1)}, u32[]{:S(2)}, u32[]{:S(2)}) collective-permute-start(bf16[128,512]{1,0:T(8,128)(2,1)S(1)} %slice.59), channel_id=1, source_target_pairs={{0,8},{1,9},{2,10},{3,11},{4,12},{5,13},{6,14},{7,15},{8,0},{9,1},... | collective-permute-start | bytes 393224 | tf_op jit(solution)/shard_map/ppermute | solution.py:15
  365.5 50.1 %collective-permute-start.2 = (bf16[256,8192]{1,0:T(8,128)(2,1)}, bf16[256,8192]{1,0:T(8,128)(2,1)S(1)}, u32[]{:S(2)}, u32[]{:S(2)}) collective-permute-start(bf16[256,8192]{1,0:T(8,128)(2,1)} %fusion.37), channel_id=1, source_target_pairs={{16,0},{32,16},{48,32},{64,48},{80,64},{96,80},{112,96},{17,1},{33... | collective-permute-start | bytes 12582920 | tf_op jit(solution)/shard_map/ppermute | solution.py:21
Sparse Core Ops, SparseCore 0:
  9.5 47.1 all-gather.6
  58.8 70.8 all-gather.8
  184.4 73.1 reduce-scatter.1
  259.8 90.8 all-gather.10
where the time goes:
time: 425 us; the launch traced here: 424 us
  waiting for transfers between devices  269 us (63%)
  matrix products  68.8 us (16%)
  local copies, waits for them, and re-layouts  49.3 us (12%)
  between operations  14.6 us (3%)
  other arithmetic  13 us (3%)
  starting transfers between devices  8.38 us (2%)
    all_gather x1, waiting for transfers between devices, body(): lax.all_gather(in_weight, 'ctx', axis=0, tiled=True)  89.8 us
    reduce_scatter x1, waiting for transfers between devices, body(): lax.psum_scatter(key_terms.reshape(seq_len, 2 * head_dim).astype(jnp.bflo...  63 us
    ppermute x1, waiting for transfers between devices, passed_along_2(): return lax.ppermute(value, axis, pairs)  47.5 us
    all_gather x1, waiting for transfers between devices, body(): gathered = lax.all_gather(stored_keyval, 'ctx', axis=0, tiled=True)  42.2 us
    dot_general x25, matrix products, contract_cols(): lax.dot_general(left_rows, right_rows, (((1,), (1,)), ((), ())), preferre...  29.2 us
    dot_general x8, matrix products, running_total(): jnp.dot(weights, value_wide, precision=lax.Precision.HIGHEST)  19.4 us
    all_gather x1, waiting for transfers between devices, body(): lax.all_gather(out_weight, 'ctx', axis=0, tiled=True)  18.4 us
    squeeze x16, local copies, waits for them, and re-layouts, body(): lax.scan(running_total, start_carry, key_blocks)  15.7 us
  transfers between devices with their start and end apart: 7, of which 7 were waited for; matrix products, arithmetic and copies ran while one was open for 13% of the time, Pallas kernels for 0%

commit v1 on v0

--- a/solution.py
+++ b/solution.py
@@ -126,7 +126,9 @@
     ).astype(jnp.bfloat16)
     local_out_grad = seq_to_stored(out_grad, block_order, device, ctx_size, per_device)
     query_positions = (block_order[:, None] * BLOCK + within[None, :]).reshape(-1)
-    gathered = lax.all_gather(stored_keyval, "ctx", axis=0, tiled=True)
+    gathered = jnp.concatenate(
+        lax.all_to_all(jnp.stack([stored_keyval] * lax.axis_size("ctx")), "ctx", 0, 0), axis=0
+    )
     slot_ids = jnp.arange(block_count, dtype=jnp.int32)
     inverse = jnp.sum(
         jnp.where(block_order[None, :] == slot_ids[:, None], slot_ids[None, :], 0), axis=1

time: 425 us -> 403 us (0.948)
  waiting for transfers between devices: 269 us -> 246 us
    all_gather x1 -> x0, waiting for transfers between devices: 42.2 us -> none  [body(): gathered = lax.all_gather(stored_keyval, 'ctx', axis=0, tiled=True)]
    all_to_all x0 -> x1, waiting for transfers between devices: none -> 35.5 us  [body(): lax.all_to_all(jnp.stack([stored_keyval] * lax.axis_size('ctx')), 'ctx',...]
    all_gather x1, waiting for transfers between devices: 18.4 us -> 0.01 us  [body(): lax.all_gather(out_weight, 'ctx', axis=0, tiled=True)]
    all_to_all x0 -> x1, starting transfers between devices: none -> 7.72 us  [body(): lax.all_to_all(jnp.stack([stored_keyval] * lax.axis_size('ctx')), 'ctx',...]
    ppermute x2, starting transfers between devices: 5.69 us -> 0.92 us  [passed_along(): return lax.ppermute(value, axis, pairs)]
  transfers between devices with their start and end apart: 7 -> 7, of which waited for: 7 -> 6; matrix products, arithmetic and copies ran while one was open for 13% -> 13% of each run, Pallas kernels for 0% -> 0%
where the time goes in v1:
time: 403 us; the launch traced here: 402 us
  waiting for transfers between devices  246 us (61%)
  matrix products  68.4 us (17%)
  local copies, waits for them, and re-layouts  48.6 us (12%)
  between operations  14.8 us (4%)
  starting transfers between devices  11.3 us (3%)
  other arithmetic  11 us (3%)
    all_gather x1, waiting for transfers between devices, body(): lax.all_gather(in_weight, 'ctx', axis=0, tiled=True)  90 us
    reduce_scatter x1, waiting for transfers between devices, body(): lax.psum_scatter(key_terms.reshape(seq_len, 2 * head_dim).astype(jnp.bflo...  62.1 us
    ppermute x1, waiting for transfers between devices, passed_along_2(): return lax.ppermute(value, axis, pairs)  47.5 us
    all_to_all x1, waiting for transfers between devices, body(): lax.all_to_all(jnp.stack([stored_keyval] * lax.axis_size('ctx')), 'ctx',...  35.5 us
    dot_general x25, matrix products, contract_cols(): lax.dot_general(left_rows, right_rows, (((1,), (1,)), ((), ())), preferre...  29.1 us
    dot_general x8, matrix products, running_total(): jnp.dot(weights, value_wide, precision=lax.Precision.HIGHEST)  19.2 us
    squeeze x16, local copies, waits for them, and re-layouts, body(): lax.scan(running_total, start_carry, key_blocks)  15.6 us
    ppermute x2, waiting for transfers between devices, passed_along(): return lax.ppermute(value, axis, pairs)  9.82 us
  transfers between devices with their start and end apart: 7, of which 6 were waited for; matrix products, arithmetic and copies ran while one was open for 13% of the time, Pallas kernels for 0%

profile of v1, /device:TPU:1, one launch (start us, length us, event | category | flops | bytes accessed | tf_op | source)
XLA Modules:
  0.0 402.0 jit_solution(5406074661522767499)
XLA Ops:
  7.3 2.5 stack.21
  9.7 7.7 %all-to-all-start = ((bf16[16,256,256]{2,1,0:T(8,128)(2,1)}), bf16[16,256,256]{2,1,0:T(8,128)(2,1)S(1)}, u32[]{:S(2)}, u32[]{:S(2)}) async-start(bf16[16,256,256]{2,1,0:T(8,128)(2,1)} %stack.21), calls=%async_computation | async-start | bytes 4194304 | tf_op jit(solution)/shard_map/all_to_all | solution.py:130
  20.5 35.5 %all-to-all-done = bf16[16,256,256]{2,1,0:T(8,128)(2,1)S(1)} async-done(((bf16[16,256,256]{2,1,0:T(8,128)(2,1)}), bf16[16,256,256]{2,1,0:T(8,128)(2,1)S(1)}, u32[]{:S(2)}, u32[]{:S(2)}) %all-to-all-start) | async-done | bytes 2097184 | tf_op jit(solution)/shard_map/all_to_all | solution.py:130
  56.1 2.0 gather_fusion
  58.1 50.7 %while.28 = (s32[]{:T(128)}, f32[1024]{0:T(1024)S(1)}, f32[1024]{0:T(1024)S(1)}, f32[1024,128]{1,0:T(8,128)}, s32[8,512]{1,0:T(8,128)S(1)}, /*index=5*/s32[8,512...) while((s32[]{:T(128)}, f32[1024]{0:T(1024)S(1)}, ...), condition=%wide.region_7.8_spmd.clone, body=%wide.region_4.7_spmd.clone.sunk | while | flops 949883904 | bytes 12720321 | solution.py:176
  58.1 1.0 dynamic-slice_bitcast_fusion.6
  61.2 2.4 convolution_add_fusion.4
  64.4 1.0 dynamic-slice_bitcast_fusion.6
  67.5 2.4 convolution_add_fusion.4
  70.8 1.0 dynamic-slice_bitcast_fusion.6
  73.9 2.4 convolution_add_fusion.4
  77.1 1.0 dynamic-slice_bitcast_fusion.6
  80.2 2.4 convolution_add_fusion.4
  83.4 1.0 dynamic-slice_bitcast_fusion.6
  86.5 2.4 convolution_add_fusion.4
  89.8 1.0 dynamic-slice_bitcast_fusion.6
  92.9 2.4 convolution_add_fusion.4
  96.1 1.0 dynamic-slice_bitcast_fusion.6
  99.2 2.4 convolution_add_fusion.4
  102.4 1.0 dynamic-slice_bitcast_fusion.6
  105.5 2.4 convolution_add_fusion.4
  108.8 7.0 %fusion.43 = bf16[256,512]{1,0:T(8,128)(2,1)S(1)} fusion(bf16[1,8192,512]{2,1,0:T(8,128)(2,1)} %all-gather.5.cloned.1.call-done, bf16[1,256,8192]{2,1,0:T(8,128)(2,1)} %param.11), kind=kOutput, calls=%fused_computation.55 | convolution fusion | flops 2147614720 | bytes 12845056 | tf_op jit(solution)/shard_map/dot_general | solution.py:122
  116.2 5.0 %collective-permute-done = bf16[128,512]{1,0:T(8,128)(2,1)S(1)} collective-permute-done((bf16[128,512]{1,0:T(8,128)(2,1)S(1)}, bf16[128,512]{1,0:T(8,128)(2,1)S(1)}, u32[]{:S(2)}, u32[]{:S(2)}) %collective-permute-start) | collective-permute-done | bytes 131104 | tf_op jit(solution)/shard_map/ppermute | solution.py:15
  121.8 40.8 %while.29 = (s32[]{:T(128)}, f32[1024,128]{1,0:T(8,128)S(1)}, bf16[8,512,256]{2,1,0:T(8,128)(2,1)}, s32[8,512]{1,0:T(8,128)S(1)}, s32[8,512]{1,0:T(8,128)S(1)}, ...) while((s32[]{:T(128)}, f32[1024,128]{1,0:T(8,128)S(1)}, ...), condition=%wide.region_10.11_spmd.clone, body=%wide.region_9.10_spmd.clone.sunk | while | flops 677642240 | bytes 14342807 | solution.py:198
  164.0 2.4 fusion.49
  167.3 4.8 %collective-permute-done.1 = bf16[128,512]{1,0:T(8,128)(2,1)S(1)} collective-permute-done((bf16[128,512]{1,0:T(8,128)(2,1)S(1)}, bf16[128,512]{1,0:T(8,128)(2,1)S(1)}, u32[]{:S(2)}, u32[]{:S(2)}) %collective-permute-start.1) | collective-permute-done | bytes 131104 | tf_op jit(solution)/shard_map/ppermute | solution.py:15
  173.1 62.1 %reduce-scatter.2.cloned.1.call-done = bf16[256,256]{1,0:T(8,128)(2,1)} async-done(((bf16[4096,256]{1,0:T(8,128)(2,1)}), bf16[256,256]{1,0:T(8,128)(2,1)}) %reduce-scatter.2.cloned.1.call-update) | async-done | bytes 131088 | tf_op jit(solution)/shard_map/reduce_scatter | solution.py:202
  238.5 90.0 %all-gather.7.cloned.1.call-done = bf16[1,8192,768]{2,1,0:T(8,128)(2,1)} async-done(((bf16[1,512,768]{2,1,0:T(8,128)(2,1)}), bf16[1,8192,768]{2,1,0:T(8,128)(2,1)}) %all-gather.7.cloned.1.call-update) | async-done | bytes 12582928 | tf_op jit(solution)/shard_map/all_gather | solution.py:217
  328.5 14.8 %fusion.37 = bf16[256,8192]{1,0:T(8,128)(2,1)} fusion(bf16[1,8192,768]{2,1,0:T(8,128)(2,1)} %all-gather.7.cloned.1.call-done, bf16[1,256,8192]{2,1,0:T(8,128)(2,1)} %param.11, bf16[256,128]{1,0:T(8,128)(2,1)S(1)} %slice.80, bf16[256,128]{1,0:T(8,128)(2,1)S(1)} %fusion.57, bf16[256,512]{1,0:T(8,128)(2,1)S(1)} %bitcast.124), kind=kOutput, calls=%fused_computation.50 | convolution fusion | flops 3228696576 | bytes 21364736 | tf_op jit(solution)/shard_map/dot_general | solution.py:90
  343.3 2.6 collective-permute-start.2
  345.9 47.5 %collective-permute-done.2 = bf16[256,8192]{1,0:T(8,128)(2,1)S(1)} collective-permute-done((bf16[256,8192]{1,0:T(8,128)(2,1)}, bf16[256,8192]{1,0:T(8,128)(2,1)S(1)}, u32[]{:S(2)}, u32[]{:S(2)}) %collective-permute-start.2) | collective-permute-done | bytes 4194336 | tf_op jit(solution)/shard_map/ppermute | solution.py:21
  393.4 2.0 copy.44
  (284 shorter events, 72.7 us)
Async XLA Ops:
  6.5 102.2 %all-gather.5.cloned.1.call-start = ((), (), s32[]{:S(2)}) async-start(), calls=%async_computation.3 | async-start | bytes 8912896 | tf_op jit(solution)/shard_map/all_gather | solution.py:124
  9.7 7.8 %copy-start.4 = (s32[1,32]{1,0:T(1,128)S(1)}, s32[1,32]{1,0:T(1,128)}, u32[]{:S(2)}) copy-start(s32[1,32]{1,0:T(1,128)} %param.17) | copy-start | bytes 388
  9.7 9.9 %copy-start.5 = (s32[1,8]{1,0:T(1,128)S(1)}, s32[1,8]{1,0:T(1,128)}, u32[]{:S(2)}) copy-start(s32[1,8]{1,0:T(1,128)} %param.16) | copy-start | bytes 100
  9.7 10.2 %copy-start.3 = (bf16[1,256,512]{2,1,0:T(8,128)(2,1)S(1)}, bf16[1,256,512]{2,1,0:T(8,128)(2,1)}, u32[]{:S(2)}) copy-start(bf16[1,256,512]{2,1,0:T(8,128)(2,1)} %param.12) | copy-start | bytes 786436
  9.7 46.3 %all-to-all-start = ((bf16[16,256,256]{2,1,0:T(8,128)(2,1)}), bf16[16,256,256]{2,1,0:T(8,128)(2,1)S(1)}, u32[]{:S(2)}, u32[]{:S(2)}) async-start(bf16[16,256,256]{2,1,0:T(8,128)(2,1)} %stack.21), calls=%async_computation | async-start | bytes 4194304 | tf_op jit(solution)/shard_map/all_to_all | solution.py:130
  17.4 217.8 %reduce-scatter.2.cloned.1.call-start = ((), (), s32[]{:S(2)}) async-start(), calls=%async_computation.2 | async-start | bytes 2228224 | tf_op jit(solution)/shard_map/reduce_scatter | solution.py:202
  60.2 1.0 copy-start
  63.6 0.8 copy-start.1
  66.5 1.0 copy-start
  69.9 0.8 copy-start.1
  72.8 1.1 copy-start
  76.3 0.8 copy-start.1
  79.2 1.0 copy-start
  82.6 0.8 copy-start.1
  85.5 1.0 copy-start
  88.9 0.8 copy-start.1
  91.8 1.0 copy-start
  95.3 0.8 copy-start.1
  98.2 1.0 copy-start
  101.6 0.8 copy-start.1
  104.5 1.0 copy-start
  107.9 0.8 copy-start.1
  108.8 12.7 %copy-start.2 = (f32[1024,128]{1,0:T(8,128)S(1)}, f32[1024,128]{1,0:T(8,128)}, u32[]{:S(2)}) copy-start(f32[1024,128]{1,0:T(8,128)} %get-tuple-element.124) | copy-start | bytes 1572868
  115.8 5.4 %collective-permute-start = (bf16[128,512]{1,0:T(8,128)(2,1)S(1)}, bf16[128,512]{1,0:T(8,128)(2,1)S(1)}, u32[]{:S(2)}, u32[]{:S(2)}) collective-permute-start(bf16[128,512]{1,0:T(8,128)(2,1)S(1)} %get-tuple-element.270), channel_id=1, source_target_pairs={{0,8},{1,9},{2,10},{3,11},{4,12},{5,13},{6,14},{7,15},{8,0},{9,1},... | collective-permute-start | bytes 393224 | tf_op jit(solution)/shard_map/ppermute | solution.py:15
  162.6 165.8 %all-gather.7.cloned.1.call-start = ((), (), s32[]{:S(2)}) async-start(), calls=%async_computation.4 | async-start | bytes 13369344 | tf_op jit(solution)/shard_map/all_gather | solution.py:217
  166.5 5.6 %collective-permute-start.1 = (bf16[128,512]{1,0:T(8,128)(2,1)S(1)}, bf16[128,512]{1,0:T(8,128)(2,1)S(1)}, u32[]{:S(2)}, u32[]{:S(2)}) collective-permute-start(bf16[128,512]{1,0:T(8,128)(2,1)S(1)} %slice.59), channel_id=1, source_target_pairs={{0,8},{1,9},{2,10},{3,11},{4,12},{5,13},{6,14},{7,15},{8,0},{9,1},... | collective-permute-start | bytes 393224 | tf_op jit(solution)/shard_map/ppermute | solution.py:15
  343.3 50.1 %collective-permute-start.2 = (bf16[256,8192]{1,0:T(8,128)(2,1)}, bf16[256,8192]{1,0:T(8,128)(2,1)S(1)}, u32[]{:S(2)}, u32[]{:S(2)}) collective-permute-start(bf16[256,8192]{1,0:T(8,128)(2,1)} %fusion.37), channel_id=1, source_target_pairs={{16,0},{32,16},{48,32},{64,48},{80,64},{96,80},{112,96},{17,1},{33... | collective-permute-start | bytes 12582920 | tf_op jit(solution)/shard_map/ppermute | solution.py:21
Sparse Core Ops, SparseCore 0:
  9.5 90.3 all-gather.4
  162.8 72.4 reduce-scatter.1
  237.6 90.8 all-gather.6
